TPU v7x, 32 devices: a whole 2x2x4 slice. The times are simulated.
32 devices in a mesh: pool: 8 (over z, x), col: 4 (over y, core).
Axes of the slice: x: 2, y: 2, z: 4, core: 2. Of those that a mesh axis runs over, the one named last changes fastest.
Arguments:
- elements: float32 [8, 128, 2048], P('pool', None, 'col'), may hold values from -6 to 6
- index_map: int32 [8, 2048], P('pool', 'col'), may hold values from 0 to 2047, as said below
- band_energy: float32 [8], P('pool'), may hold values from 0.5 to 3
- eval_energy: float32 [2], replicated, may hold values from -1 to 1
- pole_strength: float32 [2048, 2048], P(None, 'col'), may hold values from -0.0078125 to 0.0078125
- pole_frequency: float32 [2048, 2048], P(None, 'col'), may hold values from 0.5 to 4
Outputs:
- sigma: float32 [2, 128, 128], replicated
Inputs may be any that keep to these rules, and one draw needn't show every extreme that they name: For every band, the entries of index_map in columns c * 512 to (c + 1) * 512 - 1 are those same indices in some order, for every column group c.
All inputs are finite; a program needn't handle non-finite values.
Results may differ from a plain program's by a relative error of at most 0.0003.
Values sent between devices are 32-bit elements; how exact they have to be, the bound alone decides.
No kernel may reach another device: no remote copies, remote signals or barrier semaphores. Data moves between devices by JAX's collectives and lax.ppermute only.
A program may use at most 64 MiB of HBM per device.

v0:
```python
import jax
import jax.numpy as jnp
from jax import lax
from jax.sharding import PartitionSpec as P

broadening = 0.5


def mix_rows(band_rows, pole_weight, pole_frequency, eval_energy, band_level):
    highest = lax.Precision.HIGHEST
    results = []
    for energy in range(eval_energy.shape[0]):
        offset = eval_energy[energy] - band_level - pole_frequency
        tile_now = pole_weight * offset / (offset * offset + broadening * broadening)
        results.append(
            jnp.dot(band_rows, tile_now, precision=highest, preferred_element_type=jnp.float32)
        )
    return jnp.concatenate(results, axis=1)


def permute_band(band_rows, band_index_row):
    highest = lax.Precision.HIGHEST
    columns = band_rows.shape[-1]
    source = lax.broadcasted_iota(jnp.int32, (columns, columns), 0)
    selector = (band_index_row[None, :] == source).astype(jnp.float32)
    return jnp.dot(band_rows, selector, precision=highest, preferred_element_type=jnp.float32)


def local(elements, index_map, band_energy, eval_energy, pole_strength, pole_frequency):
    highest = lax.Precision.HIGHEST
    states = elements.shape[1]
    columns = elements.shape[2]
    energies = eval_energy.shape[0]
    column_group = lax.axis_index("col")
    local_index = index_map - column_group * columns
    ordered = jnp.stack([permute_band(elements[0], local_index[0])])
    pole_weight = pole_strength / (2.0 * pole_frequency)
    mixed_list = mix_rows(
        lax.all_gather(ordered[0], "col", axis=1, tiled=True),
        pole_weight,
        pole_frequency,
        eval_energy,
        band_energy[0],
    )
    shaped = mixed_list.reshape(states, energies, columns)
    local_sigma = jnp.einsum("mej,nj->emn", shaped, ordered[0], precision=highest)
    result = lax.psum(local_sigma, ("pool", "col"))
    return result


def solution(mesh):
    placed = (
        P("pool", None, "col"),
        P("pool", "col"),
        P("pool"),
        P(),
        P(None, "col"),
        P(None, "col"),
    )
    return jax.shard_map(local, mesh=mesh, in_specs=placed, out_specs=P(), check_vma=False)
```

profile of v0, /device:TPU:0, one launch (start us, length us, event | category | flops | bytes accessed | tf_op | source)
XLA Modules:
  0.0 174.7 jit_solution(7117824040149415541)
XLA Ops:
  6.5 0.0 copy-start
  6.5 0.0 all-gather.2.cloned.1.call-start
  6.5 0.7 broadcast_subtract_fusion
  7.3 0.2 copy-done
  7.5 1.4 fusion.9
  8.9 0.0 all-gather.2.cloned.1.call-update
  8.9 0.0 all-reduce.2.cloned.1.call-start
  9.6 1.3 fusion.20
  12.2 16.3 %all-gather.2.cloned.1.call-done = f32[128,2048]{0,1:T(8,128)} async-done(((f32[128,512]{0,1:T(8,128)}), f32[128,2048]{0,1:T(8,128)}) %all-gather.2.cloned.1.call-update) | async-done | bytes 1048592 | tf_op jit(solution)/shard_map/all_gather | solution.py:39
  28.5 0.0 copy-start.2
  28.5 0.0 copy-start.3
  28.5 0.0 copy-start.4
  28.5 7.7 %fusion.1 = f32[128,512]{1,0:T(8,128)S(1)} fusion(f32[128,2048]{0,1:T(8,128)} %all-gather.2.cloned.1.call-done, f32[2048,512]{1,0:T(8,128)} %param.11, f32[2048,512]{1,0:T(8,128)} %param.10, f32[]{:T(128)} %bitcast.5), kind=kOutput, calls=%fused_computation.4 | convolution fusion | flops 1617952768 | bytes 9699332 | tf_op jit(solution)/shard_map/dot_general | solution.py:16
  36.2 0.0 copy-done.2
  36.3 0.0 copy-done.3
  36.3 0.0 copy-done.4
  36.3 0.0 copy-start.1
  36.3 3.9 %fusion = f32[128,512]{1,0:T(8,128)S(1)} fusion(f32[128,2048]{0,1:T(8,128)S(1)} %copy-done.4, f32[2048,512]{1,0:T(8,128)S(1)} %copy-done.2, f32[2048,512]{1,0:T(8,128)S(1)} %copy-done.3, f32[]{:T(128)} %bitcast.4), kind=kOutput, calls=%fused_computation.3 | convolution fusion | flops 1617952768 | bytes 9699332 | tf_op jit(solution)/shard_map/dot_general | solution.py:16
  40.3 0.0 copy-done.1
  40.3 1.3 convolution_bitcast_fusion
  41.5 0.0 all-reduce.2.cloned.1.call-update
  41.6 124.6 %all-reduce.2.cloned.1.call-done = f32[2,128,128]{1,2,0:T(8,128)} async-done(((f32[2,128,128]{1,2,0:T(8,128)}), f32[2,128,128]{1,2,0:T(8,128)}) %all-reduce.2.cloned.1.call-update) | async-done | bytes 131088 | tf_op jit(solution)/shard_map/psum | solution.py:47
  166.2 1.7 copy.9
  (1 shorter events, 0.0 us)
Async XLA Ops:
  6.5 1.0 copy-start
  6.5 22.0 %all-gather.2.cloned.1.call-start = ((), (), s32[]{:S(2)}) async-start(), calls=%async_computation | async-start | bytes 1310720 | tf_op jit(solution)/shard_map/all_gather | solution.py:39
  8.9 157.2 %all-reduce.2.cloned.1.call-start = ((), (), s32[]{:S(2)}) async-start(), calls=%async_computation.1 | async-start | bytes 262144 | tf_op jit(solution)/shard_map/psum | solution.py:47
  28.5 7.7 %copy-start.2 = (f32[2048,512]{1,0:T(8,128)S(1)}, f32[2048,512]{1,0:T(8,128)}, u32[]{:S(2)}) copy-start(f32[2048,512]{1,0:T(8,128)} %param.11) | copy-start | bytes 12582916
  28.5 7.7 %copy-start.3 = (f32[2048,512]{1,0:T(8,128)S(1)}, f32[2048,512]{1,0:T(8,128)}, u32[]{:S(2)}) copy-start(f32[2048,512]{1,0:T(8,128)} %param.10) | copy-start | bytes 12582916
  28.5 7.7 %copy-start.4 = (f32[128,2048]{0,1:T(8,128)S(1)}, f32[128,2048]{0,1:T(8,128)}, u32[]{:S(2)}) copy-start(f32[128,2048]{0,1:T(8,128)} %all-gather.2.cloned.1.call-done) | copy-start | bytes 3145732
  36.3 4.0 %copy-start.1 = (f32[512,128]{1,0:T(8,128)S(1)}, f32[512,128]{1,0:T(8,128)}, u32[]{:S(2)}) copy-start(f32[512,128]{1,0:T(8,128)} %fusion.9) | copy-start | bytes 786436
Sparse Core Ops, SparseCore 0:
  9.1 19.4 all-gather.1
  41.7 124.4 all-reduce.1
where the time goes:
time: 175 us
  waiting for transfers between devices  141 us (81%)
  between operations  15.4 us (9%)
  matrix products  14.3 us (8%)
  local copies, waits for them, and re-layouts  3.24 us (2%)
    psum x1, waiting for transfers between devices, local(): result = lax.psum(local_sigma, ('pool', 'col'))  125 us
    all_gather x1, waiting for transfers between devices, local(): lax.all_gather(ordered[0], 'col', axis=1, tiled=True)  16.3 us
    dot_general x2, matrix products, mix_rows(): jnp.dot(band_rows, tile_now, precision=highest, preferred_element_type=jn...  11.6 us
  transfers between devices with their start and end apart: 2, of which 2 were waited for; matrix products, arithmetic and copies ran while one was open for 1% of the time, Pallas kernels for 0%

commit v1 on v0

--- a/solution.py
+++ b/solution.py
@@ -44,7 +44,7 @@
     )
     shaped = mixed_list.reshape(states, energies, columns)
     local_sigma = jnp.einsum("mej,nj->emn", shaped, ordered[0], precision=highest)
-    result = lax.psum(local_sigma, ("pool", "col"))
+    result = jnp.sum(lax.all_gather(local_sigma, ("pool", "col")), axis=0)
     return result
 
 

time: 175 us -> 114 us (0.65)
  waiting for transfers between devices: 141 us -> 78.1 us
  other arithmetic: 0.76 us -> 3.81 us
    psum x1 -> x0, waiting for transfers between devices: 125 us -> none  [local(): result = lax.psum(local_sigma, ('pool', 'col'))]
    all_gather x0 -> x1, waiting for transfers between devices: none -> 61.8 us  [local(): result = jnp.sum(lax.all_gather(local_sigma, ('pool', 'col')), axis=0)]
    reduce_sum x0 -> x1, other arithmetic: none -> 3.05 us  [local(): result = jnp.sum(lax.all_gather(local_sigma, ('pool', 'col')), axis=0)]
where the time goes in v1:
time: 114 us; the launch traced here: 113 us
  waiting for transfers between devices  78.1 us (69%)
  between operations  15.4 us (14%)
  matrix products  13.7 us (12%)
  other arithmetic  3.81 us (3%)
  local copies, waits for them, and re-layouts  2.34 us (2%)
    all_gather x1, waiting for transfers between devices, local(): result = jnp.sum(lax.all_gather(local_sigma, ('pool', 'col')), axis=0)  61.8 us
    all_gather x1, waiting for transfers between devices, local(): lax.all_gather(ordered[0], 'col', axis=1, tiled=True)  16.3 us
    dot_general x2, matrix products, mix_rows(): jnp.dot(band_rows, tile_now, precision=highest, preferred_element_type=jn...  11.6 us
    reduce_sum x1, other arithmetic, local(): result = jnp.sum(lax.all_gather(local_sigma, ('pool', 'col')), axis=0)  3.05 us
  transfers between devices with their start and end apart: 2, of which 2 were waited for; matrix products, arithmetic and copies ran while one was open for 1% of the time, Pallas kernels for 0%

profile of v1, /device:TPU:0, one launch (start us, length us, event | category | flops | bytes accessed | tf_op | source)
XLA Modules:
  0.0 113.3 jit_solution(5356710826908374951)
XLA Ops:
  6.5 0.0 copy-start
  6.5 0.0 all-gather.4.cloned.1.call-start
  6.5 0.7 broadcast_subtract_fusion
  7.3 0.2 copy-done
  7.5 1.4 %fusion.9 = f32[512,128]{1,0:T(8,128)} fusion(s32[512]{0:T(512)S(1)} %bitcast.22, f32[1,128,512]{2,1,0:T(8,128)S(1)} %copy-done), kind=kOutput, calls=%fused_computation.14 | convolution fusion | flops 403177472 | bytes 526336 | tf_op jit(solution)/shard_map/dot_general | solution.py:26
  8.9 0.0 all-gather.4.cloned.1.call-update
  8.9 0.0 all-gather.6.cloned.1.call-start
  9.6 1.3 %fusion.20 = (f32[1]{0:T(128)}, f32[1]{0:T(128)}) fusion(f32[2]{0:T(128)} %param.9), kind=kLoop, calls=%fused_computation.26 | loop fusion | bytes 16 | tf_op jit(solution)/shard_map/slice | solution.py:13
  12.2 16.3 %all-gather.4.cloned.1.call-done = f32[128,2048]{0,1:T(8,128)} async-done(((f32[128,512]{0,1:T(8,128)}), f32[128,2048]{0,1:T(8,128)}) %all-gather.4.cloned.1.call-update) | async-done | bytes 1048592 | tf_op jit(solution)/shard_map/all_gather | solution.py:39
  28.5 0.0 copy-start.2
  28.5 0.0 copy-start.3
  28.5 0.0 copy-start.4
  28.5 7.7 %fusion.1 = f32[128,512]{1,0:T(8,128)S(1)} fusion(f32[128,2048]{0,1:T(8,128)} %all-gather.4.cloned.1.call-done, f32[2048,512]{1,0:T(8,128)} %param.11, f32[2048,512]{1,0:T(8,128)} %param.10, f32[]{:T(128)} %bitcast.5), kind=kOutput, calls=%fused_computation.4 | convolution fusion | flops 1617952768 | bytes 9699332 | tf_op jit(solution)/shard_map/dot_general | solution.py:16
  36.2 0.0 copy-done.2
  36.3 0.0 copy-done.3
  36.3 0.0 copy-done.4
  36.3 0.0 copy-start.1
  36.3 3.9 %fusion = f32[128,512]{1,0:T(8,128)S(1)} fusion(f32[128,2048]{0,1:T(8,128)S(1)} %copy-done.4, f32[2048,512]{1,0:T(8,128)S(1)} %copy-done.2, f32[2048,512]{1,0:T(8,128)S(1)} %copy-done.3, f32[]{:T(128)} %bitcast.4), kind=kOutput, calls=%fused_computation.3 | convolution fusion | flops 1617952768 | bytes 9699332 | tf_op jit(solution)/shard_map/dot_general | solution.py:16
  40.3 0.0 copy-done.1
  40.3 0.6 convolution_bitcast_fusion
  40.9 0.8 copy.11
  41.6 0.0 all-gather.6.cloned.1.call-update
  41.7 61.8 %all-gather.6.cloned.1.call-done = f32[64,128,128]{2,1,0:T(8,128)} async-done(((f32[2,128,128]{2,1,0:T(8,128)}), f32[64,128,128]{2,1,0:T(8,128)}) %all-gather.6.cloned.1.call-update) | async-done | bytes 4194320 | tf_op jit(solution)/shard_map/all_gather | solution.py:47
  103.4 3.0 %reduce_sum.9 = f32[2,128,128]{2,1,0:T(8,128)} reduce(f32[32,2,128,128]{3,2,1,0:T(8,128)} %bitcast.19, f32[]{:T(128)} %constant.4.clone.1), dimensions={0}, to_apply=%region_0.0 | reduce | flops 1015808 | bytes 4325380 | tf_op jit(solution)/shard_map/reduce_sum | solution.py:47
  (1 shorter events, 0.0 us)
Async XLA Ops:
  6.5 1.0 copy-start
  6.5 22.0 %all-gather.4.cloned.1.call-start = ((), (), s32[]{:S(2)}) async-start(), calls=%async_computation | async-start | bytes 1310720 | tf_op jit(solution)/shard_map/all_gather | solution.py:39
  8.9 94.5 %all-gather.6.cloned.1.call-start = ((), (), s32[]{:S(2)}) async-start(), calls=%async_computation.1 | async-start | bytes 4325376 | tf_op jit(solution)/shard_map/all_gather | solution.py:47
  28.5 7.7 %copy-start.2 = (f32[2048,512]{1,0:T(8,128)S(1)}, f32[2048,512]{1,0:T(8,128)}, u32[]{:S(2)}) copy-start(f32[2048,512]{1,0:T(8,128)} %param.11) | copy-start | bytes 12582916
  28.5 7.7 %copy-start.3 = (f32[2048,512]{1,0:T(8,128)S(1)}, f32[2048,512]{1,0:T(8,128)}, u32[]{:S(2)}) copy-start(f32[2048,512]{1,0:T(8,128)} %param.10) | copy-start | bytes 12582916
  28.5 7.7 %copy-start.4 = (f32[128,2048]{0,1:T(8,128)S(1)}, f32[128,2048]{0,1:T(8,128)}, u32[]{:S(2)}) copy-start(f32[128,2048]{0,1:T(8,128)} %all-gather.4.cloned.1.call-done) | copy-start | bytes 3145732
  36.3 4.0 %copy-start.1 = (f32[512,128]{1,0:T(8,128)S(1)}, f32[512,128]{1,0:T(8,128)}, u32[]{:S(2)}) copy-start(f32[512,128]{1,0:T(8,128)} %fusion.9) | copy-start | bytes 786436
Sparse Core Ops, SparseCore 0:
  9.1 19.4 all-gather.3
  41.8 61.6 all-gather.5
